TPU v7x, 128 devices: a whole 4x4x4 slice. The times are simulated.
128 devices in a mesh: req: 16 (over y, z), tp: 8 (over x, core).
Axes of the slice: x: 4, y: 4, z: 4, core: 2. Of those that a mesh axis runs over, the one named last changes fastest.
Arguments:
- suffix_tokens: bfloat16 [256, 112, 2880], P('req'), may hold values from -40 to 40
- route_lengths: int32 [16, 16], replicated, may hold values from 1 to 112, 768 in all within a row
- dest_perm: int32 [16, 16], replicated, may hold values from 0 to 15, each once within a row
- attach_points: int32 [256], replicated, may hold values from 256 to 8192
- prefix_cache: bfloat16 [64, 128, 8, 128], P('req', None, 'tp'), may hold values from -120 to 120
- block_of_slot: int32 [64], replicated, may hold values from 0 to 63, each once
- sink_logits: float32 [64], P('tp'), may hold values from 0 to 6
- attn_gain: bfloat16 [2880], replicated, may hold values from 0.099609375 to 1.8984375
- w_query: bfloat16 [2880, 4096], P(None, 'tp'), may hold values from -0.109375 to 0.109375
- w_keyval: bfloat16 [2880, 8, 128], P(None, 'tp'), may hold values from -0.109375 to 0.109375
- w_out: bfloat16 [4096, 2880], P('tp'), may hold values from -0.09375 to 0.09375
- mlp_gain: bfloat16 [2880], replicated, may hold values from 0.099609375 to 1.8984375
- w_gate: bfloat16 [2880, 2880], P(None, 'tp'), may hold values from -0.109375 to 0.109375
- w_up: bfloat16 [2880, 2880], P(None, 'tp'), may hold values from -0.109375 to 0.109375
- w_down: bfloat16 [2880, 2880], P('tp'), may hold values from -0.109375 to 0.109375
Outputs:
- layer_out: bfloat16 [256, 112, 2880], P('req', None, 'tp')
Inputs may be any that keep to these rules, and one draw needn't show every extreme that they name: `route_lengths`: each row sums to 768, and the largest entry of each row is 112. `dest_perm`: each row is a permutation of the devices of req. `block_of_slot`: a permutation.
All inputs are finite; a program needn't handle non-finite values.
Results may differ from a plain program's by a relative error of at most 0.013.
Values may be sent and summed in bfloat16 or wider, within the bound.
No kernel may reach another device: no remote copies, remote signals or barrier semaphores. Data moves between devices by JAX's collectives and lax.ppermute only.
A program may use at most 192 MiB of HBM per device.

v0:
```python
import jax
import jax.numpy as jnp
from jax import lax
from jax.sharding import PartitionSpec as P

WINDOW = 128
CAP = 768
ROPE_BASE = 150000.0
EPSILON = 1e-05


def norm_rows(inputs, gains):
    widened = inputs.astype(jnp.float32)
    factor = lax.rsqrt(jnp.mean(widened * widened, axis=-1, keepdims=True) + EPSILON)
    return (widened * factor * gains.astype(jnp.float32)).astype(jnp.bfloat16)


def rotate(vectors, positions):
    half_dim = vectors.shape[-1] // 2
    frequency = ROPE_BASE ** (-(jnp.arange(half_dim).astype(jnp.float32) * 2.0 / vectors.shape[-1]))
    angles = positions.astype(jnp.float32)[:, None, None] * frequency
    cosine = jnp.cos(angles)
    sine_part = jnp.sin(angles)
    first_half = vectors[..., :half_dim]
    second = vectors[..., half_dim:]
    return jnp.concatenate(
        [first_half * cosine - second * sine_part, second * cosine + first_half * sine_part],
        axis=-1,
    )


def attend(query_slots, paired_slots, tail_rows, sink_logits):
    peers, slot_length = (query_slots.shape[0], query_slots.shape[1])
    value_heads = paired_slots.shape[2]
    head_dim = paired_slots.shape[3] // 2
    group_size = query_slots.shape[2] // value_heads
    window = tail_rows.shape[1]
    grouped_query = query_slots.reshape(peers, slot_length, value_heads, group_size, head_dim)
    near_keys = jnp.concatenate([tail_rows, paired_slots], axis=1)
    score_scale = head_dim ** (-0.5)
    near_scores = (
        jnp.einsum(
            "ntkgd,nskd->nkgts",
            grouped_query,
            near_keys[..., :head_dim],
            preferred_element_type=jnp.float32,
        )
        * score_scale
    )
    sink_scores = sink_logits.reshape(value_heads, group_size)[None, :, :, None, None]
    slot_steps = jnp.arange(slot_length)
    columns = jnp.arange(window + slot_length)
    allowed = jnp.where(
        columns[None, :] < window,
        columns[None, :] > slot_steps[:, None],
        columns[None, :] - window <= slot_steps[:, None],
    )
    near_scores = jnp.where(allowed, near_scores, -jnp.inf)
    largest = jnp.maximum(jnp.max(near_scores, axis=-1, keepdims=True), sink_scores)
    near_weights = jnp.exp(near_scores - largest)
    normalizer = jnp.sum(near_weights, axis=-1, keepdims=True) + jnp.exp(sink_scores - largest)
    near_weights = (near_weights / normalizer).astype(jnp.bfloat16)
    mixed = jnp.einsum(
        "nkgts,nskd->ntkgd",
        near_weights,
        near_keys[..., head_dim:],
        preferred_element_type=jnp.float32,
    )
    return mixed.astype(jnp.bfloat16).reshape(
        peers * slot_length, value_heads * group_size * head_dim
    )


def fetch_prefix(attach_slots, prefix_cache, block_of_slot, window):
    total_blocks = block_of_slot.shape[0]
    block_len = prefix_cache.shape[1]
    catalog = jnp.arange(total_blocks)
    home_row = jnp.sum(
        jnp.where(block_of_slot[None, :] == catalog[:, None], catalog[None, :], 0), axis=1
    )
    wanted = attach_slots[:, None] - window + jnp.arange(window)[None, :]
    block_id = wanted // block_len
    tail_store = jnp.sum(jnp.where(block_id[..., None] == catalog, home_row, 0), axis=-1)
    tail_offset = wanted - block_id * block_len
    trailing = prefix_cache.shape[2:]
    initial = jnp.zeros((attach_slots.shape[0], window) + trailing, jnp.bfloat16)
    shard_rows = lax.all_gather(prefix_cache, "req", axis=0, tiled=True)
    held_blocks = shard_rows.shape[0]
    flat_rows = shard_rows.reshape((held_blocks * block_len,) + trailing)
    inside = (tail_store >= 0) & (tail_store < held_blocks)
    picked = flat_rows[jnp.clip(tail_store, 0, held_blocks - 1) * block_len + tail_offset]
    return jnp.where(inside[..., None, None], picked, initial)


def local(
    suffix_tokens,
    route_lengths,
    dest_perm,
    attach_points,
    prefix_cache,
    block_of_slot,
    sink_logits,
    attn_gain,
    w_query,
    w_keyval,
    w_out,
    mlp_gain,
    w_gate,
    w_up,
    w_down,
):
    peers = lax.axis_size("req")
    splits = lax.axis_size("tp")
    request_index = lax.axis_index("req")
    tensor_index = lax.axis_index("tp")
    slot_count, slot_length, features = suffix_tokens.shape
    feature_share = features // splits
    value_heads = w_keyval.shape[1]
    head_dim = w_keyval.shape[2] // 2
    peer_ids = jnp.arange(peers)
    slot_steps = jnp.arange(slot_length)
    my_row = lax.dynamic_index_in_dim(dest_perm, request_index, 0, keepdims=False)
    attach_table = attach_points.reshape(peers, peers)
    arriving_lengths = lax.dynamic_index_in_dim(route_lengths, request_index, 0, keepdims=False)
    arriving = (dest_perm == request_index).astype(jnp.int32)
    arriving_attach = jnp.sum(attach_table * arriving, axis=1)
    send_order = jnp.sum(
        jnp.where(my_row[None, :] == peer_ids[:, None], peer_ids[None, :], 0), axis=1
    )
    run_ends = jnp.cumsum(arriving_lengths)
    starts = run_ends - arriving_lengths
    packed_ids = jnp.arange(CAP)
    source_of = jnp.sum((run_ends[None, :] <= packed_ids[:, None]).astype(jnp.int32), axis=1)
    source_hot = (source_of[:, None] == peer_ids[None, :]).astype(jnp.int32)
    token_index = packed_ids - jnp.sum(source_hot * starts[None, :], axis=1)
    positions = jnp.sum(source_hot * arriving_attach[None, :], axis=1) + token_index
    flat_index = source_of * slot_length + token_index
    slot_source = jnp.clip(starts[:, None] + slot_steps[None, :], 0, CAP - 1).reshape(-1)
    live_mask = slot_steps[None, :] < arriving_lengths[:, None]

    def to_slots(values):
        return values[slot_source].reshape((peers, slot_length) + values.shape[1:])

    tail_rows = fetch_prefix(arriving_attach, prefix_cache, block_of_slot, WINDOW)
    landed = lax.all_to_all(
        suffix_tokens[send_order], "req", split_axis=0, concat_axis=0, tiled=True
    )
    input_rows = landed.reshape(peers * slot_length, features)[flat_index]
    row_total = input_rows.shape[0]
    normed_in = norm_rows(input_rows, attn_gain)
    queries = jnp.dot(normed_in, w_query, preferred_element_type=jnp.float32).reshape(
        row_total, -1, head_dim
    )
    queries = rotate(queries, positions).astype(jnp.bfloat16)
    paired = jnp.dot(
        normed_in, w_keyval.reshape(features, -1), preferred_element_type=jnp.float32
    ).reshape(row_total, value_heads, 2 * head_dim)
    rotated = rotate(paired[..., :head_dim], positions)
    paired = jnp.concatenate([rotated, paired[..., head_dim:]], axis=-1).astype(jnp.bfloat16)
    attended = attend(to_slots(queries), to_slots(paired), tail_rows, sink_logits)[flat_index]
    partial_value = jnp.dot(attended, w_out, preferred_element_type=jnp.float32)
    summed = lax.psum(partial_value.astype(jnp.bfloat16), "tp").astype(jnp.float32)
    residual = (input_rows.astype(jnp.float32) + summed).astype(jnp.bfloat16)
    normed_mid = norm_rows(residual, mlp_gain)
    residual_part = lax.dynamic_slice_in_dim(
        residual, tensor_index * feature_share, feature_share, 1
    )
    gate_proj = jnp.dot(normed_mid, w_gate, preferred_element_type=jnp.float32)
    up_proj = jnp.dot(normed_mid, w_up, preferred_element_type=jnp.float32)
    hidden = (jax.nn.silu(gate_proj) * up_proj).astype(jnp.bfloat16)
    down_sum = lax.psum_scatter(
        jnp.dot(hidden, w_down, preferred_element_type=jnp.float32).astype(jnp.bfloat16),
        "tp",
        scatter_dimension=1,
        tiled=True,
    ).astype(jnp.float32)
    out_rows = (residual_part.astype(jnp.float32) + down_sum).astype(jnp.bfloat16)
    out_slots = jnp.where(live_mask[..., None], to_slots(out_rows), jnp.zeros((), jnp.bfloat16))
    returned = lax.all_to_all(out_slots, "req", split_axis=0, concat_axis=0, tiled=True)
    return returned[my_row]


def solution(mesh):
    in_specs = (
        P("req", None, None),
        P(),
        P(),
        P(),
        P("req", None, "tp", None),
        P(),
        P("tp"),
        P(),
        P(None, "tp"),
        P(None, "tp", None),
        P("tp", None),
        P(),
        P(None, "tp"),
        P(None, "tp"),
        P("tp", None),
    )
    out_specs = P("req", None, "tp")
    return jax.shard_map(local, mesh=mesh, in_specs=in_specs, out_specs=out_specs, check_vma=False)
```

profile of v0, /device:TPU:7, one launch (start us, length us, event | category | flops | bytes accessed | tf_op | source)
XLA Modules:
  0.0 531.0 jit_solution(8293416445364604269)
XLA Ops:
  6.5 0.8 fusion.62
  7.4 0.1 select_reduce_fusion.5
  7.5 9.7 %gather_fusion = bf16[16,112,2880]{2,1,0:T(8,128)(2,1)} fusion(bf16[16,112,2880]{2,1,0:T(8,128)(2,1)} %param.15, s32[1024]{0:T(1024)S(1)} %pad_clamp_fusion.3), kind=kCustom, calls=%fused_computation | custom fusion | bytes 20643904 | tf_op jit(solution)/shard_map/gather | solution.py:146
  17.2 8.0 %all-to-all-start = ((bf16[16,112,2880]{2,1,0:T(8,128)(2,1)}), bf16[16,112,2880]{2,1,0:T(8,128)(2,1)}, u32[]{:S(2)}, u32[]{:S(2)}) async-start(bf16[16,112,2880]{2,1,0:T(8,128)(2,1)} %gather_fusion), calls=%async_computation | async-start | bytes 21102592 | tf_op jit(solution)/shard_map/all_to_all | solution.py:145
  25.2 0.7 all-gather.2.cloned.1.call-update
  25.9 0.7 fusion.77
  26.6 0.1 copy.44
  26.8 0.1 reduce.2
  27.0 0.7 bitcast_subtract_fusion.1
  27.7 0.1 min.22
  27.8 0.1 select_reduce_fusion.4
  28.0 0.1 convert_reduce_fusion
  28.0 0.7 fusion.61
  28.7 0.1 select_reduce_fusion.1
  29.0 0.1 select_reduce_fusion.3
  29.1 0.1 add_select_fusion.1
  29.2 0.2 select_reduce_fusion
  29.4 0.1 fusion.52
  29.5 2.5 multiply_cosine_fusion
  32.0 176.3 %all-gather.2.cloned.1.call-done = bf16[64,128,1,128]{3,1,2,0:T(8,128)(2,1)} async-done(((bf16[4,128,1,128]{3,1,2,0:T(8,128)(2,1)}), bf16[64,128,1,128]{3,1,2,0:T(8,128)(2,1)}) %all-gather.2.cloned.1.call-update) | async-done | bytes 2097168 | tf_op jit(solution)/shard_map/all_gather | solution.py:87
  208.3 7.4 %gather_fusion.2 = bf16[2048,128]{1,0:T(8,128)(2,1)S(1)} fusion(bf16[8192,128]{1,0:T(8,128)(2,1)} %bitcast.90, s32[2048]{0:T(1024)S(1)} %fusion.52), kind=kCustom, calls=%fused_computation.2 | custom fusion | bytes 1056768 | tf_op jit(solution)/shard_map/gather | solution.py:91
  215.8 1.0 copy.46
  216.8 1.9 broadcast_select_fusion.1
  218.7 14.6 %gather_fusion.1 = bf16[768,2880]{1,0:T(8,128)(2,1)} fusion(bf16[1792,2880]{1,0:T(8,128)(2,1)} %bitcast.4, s32[1024]{0:T(1024)S(1)} %pad_clamp_fusion.2), kind=kCustom, calls=%fused_computation.1 | custom fusion | bytes 8850432 | tf_op jit(solution)/shard_map/gather | solution.py:148
  233.3 6.6 %copy.45 = bf16[768,2880]{0,1:T(8,128)(2,1)} copy(bf16[768,2880]{1,0:T(8,128)(2,1)} %gather_fusion.1) | data formatting | bytes 8847360 | tf_op jit(solution)/shard_map/gather | solution.py:148
  239.9 3.3 fusion.5
  243.3 0.2 copy-done.1
  243.5 2.6 fusion.24
  246.1 0.4 fusion.43
  246.6 0.2 copy.47
  246.8 16.1 %gather_fusion.3 = bf16[1792,128]{1,0:T(8,128)(2,1)} fusion(bf16[768,128]{1,0:T(8,128)(2,1)S(1)} %copy.47, s32[2048]{0:T(1024)S(1)} %pad_clamp_fusion), kind=kCustom, calls=%fused_computation.3 | custom fusion | bytes 924672 | tf_op jit(solution)/shard_map/gather | solution.py:142
  262.9 2.0 copy.48
  264.9 6.1 %fusion.20 = f32[768,512]{0,1:T(8,128)S(1)} fusion(bf16[2880,512]{1,0:T(8,128)(2,1)} %param.23, bf16[768,2880]{0,1:T(8,128)(2,1)} %copy.45, f32[2880]{0:T(1024)S(1)} %convert_element_type.90, f32[768]{0:T(1024)S(1)} %add_rsqrt_fusion.1), kind=kOutput, calls=%fused_computation.40 | convolution fusion | flops 2273771520 | bytes 8960256 | tf_op jit(solution)/shard_map/dot_general | solution.py:151
  271.0 1.3 fusion.69
  272.2 3.2 copy.62
  275.4 3.2 copy.63
  278.6 3.7 subtract_convert_fusion
  282.3 2.1 pad_maximum_fusion
  284.4 5.7 %gather_fusion.4 = bf16[1792,8,64]{2,1,0:T(8,128)(2,1)} fusion(bf16[768,8,64]{2,1,0:T(8,128)(2,1)} %pad_maximum_fusion, s32[2048]{0:T(1024)S(1)} %pad_clamp_fusion), kind=kCustom, calls=%fused_computation.4 | custom fusion | bytes 3677184 | tf_op jit(solution)/shard_map/gather | solution.py:142
  290.1 5.1 fusion.1
  295.4 5.3 fusion
  300.6 0.1 exponential_add_fusion
  300.7 6.6 %convert_bitcast_fusion = bf16[16,112,1,8,64]{1,4,3,0,2:T(8,128)(2,1)} fusion(f32[16,8,112]{2,1,0:T(8,128)S(1)} %exponential_add_fusion, f32[16,8,112]{2,1,0:T(8,128)S(1)} %broadcast_maximum_fusion, f32[16,240,112,8]{1,2,3,0:T(8,128)S(1)} %get-tuple-element.18, pred[112,240]{1,0:T(8,128)(4,1)S(1)} %fusion.41, bf16[16,128,1,128]{1,3,0,2:T(8,128)(2,1)S(1)} %copy-done.3, ...), kind=kOutput, calls=%fused_computation.34 | convolution fusion | flops 459505664 | bytes 16722176 | tf_op jit(solution)/shard_map/nkgts,nskd->ntkgd/dot_general | solution.py:63
  307.3 4.8 copy.60
  312.2 5.9 %reshape.650 = bf16[1792,512]{1,0:T(8,128)(2,1)} reshape(bf16[16,112,1,8,64]{4,3,1,0,2:T(8,128)(2,1)} %copy.60) | data formatting | bytes 3670016 | tf_op jit(solution)/shard_map/reshape | solution.py:69
  318.1 5.1 gather_fusion.5
  323.2 5.7 %convolution_convert_fusion = bf16[768,2880]{0,1:T(8,128)(2,1)} fusion(bf16[768,512]{1,0:T(8,128)(2,1)} %gather_fusion.5, bf16[512,2880]{0,1:T(8,128)(2,1)S(1)} %copy-done), kind=kOutput, calls=%fused_computation.28 | convolution fusion | flops 2267136000 | bytes 8159232 | tf_op jit(solution)/shard_map/dot_general | solution.py:161
  328.9 0.2 reduce-scatter.2.cloned.1.call-start
  329.1 0.4 copy-done.8
  329.6 91.0 %all-reduce.2.cloned.1.call-done = bf16[768,2880]{0,1:T(8,128)(2,1)} async-done(((bf16[768,2880]{0,1:T(8,128)(2,1)}), bf16[768,2880]{0,1:T(8,128)(2,1)}) %all-reduce.2.cloned.1.call-update) | async-done | bytes 4423696 | tf_op jit(solution)/shard_map/psum | solution.py:162
  420.6 5.5 %fusion.2 = (f32[768]{0:T(1024)S(1)}, bf16[768,2880]{0,1:T(8,128)(2,1)S(1)}) fusion(bf16[768,2880]{0,1:T(8,128)(2,1)} %all-reduce.2.cloned.1.call-done, bf16[768,2880]{0,1:T(8,128)(2,1)} %copy.45), kind=kLoop, calls=%fused_computation.18 | loop fusion | flops 15482112 | bytes 13274112 | tf_op jit(solution)/shard_map/reduce_sum | solution.py:14
  426.1 2.0 copy-done.2
  428.1 3.2 fusion.18
  431.4 11.4 %convolution_convert_fusion.1 = bf16[768,2880]{0,1:T(8,128)(2,1)} fusion(bf16[360,2880]{1,0:T(8,128)(2,1)} %param.29, bf16[2880,360]{0,1:T(8,128)(2,1)} %param.28, bf16[768,2880]{0,1:T(8,128)(2,1)} %copy-done.2, f32[2880]{0:T(1024)S(1)} %convert_element_type.103, f32[768]{0:T(1024)S(1)} %add_rsqrt_fusion, f32[768,360]{0,1:T(8,128)} %fusion.18), kind=kOutput, calls=%fused_computation.29 | convolution fusion | flops 3197767680 | bytes 14115072 | tf_op jit(solution)/shard_map/dot_general | solution.py:172
  442.7 0.7 fusion.76
  443.5 36.8 %reduce-scatter.2.cloned.1.call-done = bf16[768,360]{0,1:T(8,128)(2,1)} async-done(((bf16[768,2880]{0,1:T(8,128)(2,1)}), bf16[768,360]{0,1:T(8,128)(2,1)}) %reduce-scatter.2.cloned.1.call-update) | async-done | bytes 552976 | tf_op jit(solution)/shard_map/reduce_scatter | solution.py:171
  480.4 2.1 add_convert_fusion.1
  482.5 1.4 copy.55
  483.9 6.0 %gather_fusion.6 = bf16[1792,360]{1,0:T(8,128)(2,1)} fusion(bf16[768,360]{1,0:T(8,128)(2,1)S(1)} %copy.55, s32[2048]{0:T(1024)S(1)} %pad_clamp_fusion), kind=kCustom, calls=%fused_computation.6 | custom fusion | bytes 2587648 | tf_op jit(solution)/shard_map/gather | solution.py:142
  489.8 2.7 broadcast_select_fusion
  492.6 6.8 %all-to-all-start.1 = ((bf16[16,112,360]{2,1,0:T(8,128)(2,1)}), bf16[16,112,360]{2,1,0:T(8,128)(2,1)}, u32[]{:S(2)}, u32[]{:S(2)}) async-start(bf16[16,112,360]{2,1,0:T(8,128)(2,1)} %broadcast_select_fusion), calls=%async_computation.2 | async-start | bytes 2752512 | tf_op jit(solution)/shard_map/all_to_all | solution.py:179
  499.4 0.7 fusion.60
  500.1 20.9 %all-to-all-done.1 = bf16[16,112,360]{2,1,0:T(8,128)(2,1)} async-done(((bf16[16,112,360]{2,1,0:T(8,128)(2,1)}), bf16[16,112,360]{2,1,0:T(8,128)(2,1)}, u32[]{:S(2)}, u32[]{:S(2)}) %all-to-all-start.1) | async-done | bytes 1290272 | tf_op jit(solution)/shard_map/all_to_all | solution.py:179
  521.0 3.2 gather_fusion.7
  (54 shorter events, 0.7 us)
Async XLA Ops:
  6.5 316.6 %copy-start = (bf16[512,2880]{0,1:T(8,128)(2,1)S(1)}, bf16[512,2880]{0,1:T(8,128)(2,1)}, u32[]{:S(2)}) copy-start(bf16[512,2880]{0,1:T(8,128)(2,1)} %param.25) | copy-start | bytes 8847364
  17.2 9.7 %copy-start.10 = (s32[256]{0:T(256)S(1)}, s32[256]{0:T(256)}, u32[]{:S(2)}) copy-start(s32[256]{0:T(256)} %param.18) | copy-start | bytes 3076
  17.2 9.8 %copy-start.7 = (bf16[2880]{0:T(1024)(128)(2,1)S(1)}, bf16[2880]{0:T(1024)(128)(2,1)}, u32[]{:S(2)}) copy-start(bf16[2880]{0:T(1024)(128)(2,1)} %param.22) | copy-start | bytes 17284
  17.2 10.7 %copy-start.6 = (s32[16,16]{1,0:T(8,128)S(1)}, s32[16,16]{1,0:T(8,128)}, u32[]{:S(2)}) copy-start(s32[16,16]{1,0:T(8,128)} %param.17) | copy-start | bytes 3076
  17.2 11.8 %copy-start.12 = (s32[64]{0:T(128)S(1)}, s32[64]{0:T(128)}, u32[]{:S(2)}) copy-start(s32[64]{0:T(128)} %param.20) | copy-start | bytes 772
  17.2 201.5 %all-to-all-start = ((bf16[16,112,2880]{2,1,0:T(8,128)(2,1)}), bf16[16,112,2880]{2,1,0:T(8,128)(2,1)}, u32[]{:S(2)}, u32[]{:S(2)}) async-start(bf16[16,112,2880]{2,1,0:T(8,128)(2,1)} %gather_fusion), calls=%async_computation | async-start | bytes 21102592 | tf_op jit(solution)/shard_map/all_to_all | solution.py:145
  25.2 183.2 %all-gather.2.cloned.1.call-start = ((), (), s32[]{:S(2)}) async-start(), calls=%async_computation.3 | async-start | bytes 2228224 | tf_op jit(solution)/shard_map/all_gather | solution.py:87
  25.9 394.7 %all-reduce.2.cloned.1.call-start = ((), (), s32[]{:S(2)}) async-start(), calls=%async_computation.4 | async-start | bytes 8847360 | tf_op jit(solution)/shard_map/psum | solution.py:162
  239.9 3.6 copy-start.1
  272.2 6.4 %copy-start.5 = (f32[768,32]{1,0:T(8,128)S(1)}, f32[768,32]{1,0:T(8,128)}, u32[]{:S(2)}) copy-start(f32[768,32]{1,0:T(8,128)} %get-tuple-element.15) | copy-start | bytes 294916
  284.4 5.7 %copy-start.3 = (bf16[16,128,1,128]{1,3,0,2:T(8,128)(2,1)S(1)}, bf16[16,128,1,128]{1,3,0,2:T(8,128)(2,1)}, u32[]{:S(2)}) copy-start(bf16[16,128,1,128]{1,3,0,2:T(8,128)(2,1)} %broadcast_select_fusion.1) | copy-start | bytes 1572868
  290.1 5.1 copy-start.9
  295.4 5.4 %copy-start.4 = (bf16[16,112,1,128]{1,3,0,2:T(8,128)(2,1)S(1)}, bf16[16,112,1,128]{1,3,0,2:T(8,128)(2,1)}, u32[]{:S(2)}) copy-start(bf16[16,112,1,128]{1,3,0,2:T(8,128)(2,1)} %copy.48) | copy-start | bytes 1376260
  328.9 0.7 copy-start.8
  328.9 151.4 %reduce-scatter.2.cloned.1.call-start = ((), (), s32[]{:S(2)}) async-start(), calls=%async_computation.5 | async-start | bytes 4976640 | tf_op jit(solution)/shard_map/reduce_scatter | solution.py:171
  420.6 7.5 %copy-start.11 = (bf16[2880,360]{0,1:T(8,128)(2,1)S(1)}, bf16[2880,360]{0,1:T(8,128)(2,1)}, u32[]{:S(2)}) copy-start(bf16[2880,360]{0,1:T(8,128)(2,1)} %param.27) | copy-start | bytes 6220804
  426.1 2.0 copy-start.2
  492.6 28.4 %all-to-all-start.1 = ((bf16[16,112,360]{2,1,0:T(8,128)(2,1)}), bf16[16,112,360]{2,1,0:T(8,128)(2,1)}, u32[]{:S(2)}, u32[]{:S(2)}) async-start(bf16[16,112,360]{2,1,0:T(8,128)(2,1)} %broadcast_select_fusion), calls=%async_computation.2 | async-start | bytes 2752512 | tf_op jit(solution)/shard_map/all_to_all | solution.py:179
Sparse Core Ops, SparseCore 0:
  28.1 180.1 all-gather.1
  329.0 91.5 all-reduce.1
  442.9 37.4 reduce-scatter.1
where the time goes:
time: 540 us; the launch traced here: 531 us
  waiting for transfers between devices  326 us (60%)
  local copies, waits for them, and re-layouts  103 us (19%)
  matrix products  40.7 us (8%)
  other arithmetic  33.2 us (6%)
  starting transfers between devices  15 us (3%)
  between operations  13.8 us (3%)
    all_gather x1, waiting for transfers between devices, fetch_prefix(): shard_rows = lax.all_gather(prefix_cache, 'req', axis=0, tiled=True)  176 us
    psum x1, waiting for transfers between devices, local(): lax.psum(partial_value.astype(jnp.bfloat16), 'tp').astype(jnp.float32)  91 us
    reduce_scatter x1, waiting for transfers between devices, local(): lax.psum_scatter(jnp.dot(hidden, w_down, preferred_element_type=jnp.float...  36.8 us
    gather x3, local copies, waits for them, and re-layouts, to_slots(): return values[slot_source].reshape((peers, slot_length) + values.shape[1:])  27.8 us
    gather x2, local copies, waits for them, and re-layouts, local(): input_rows = landed.reshape(peers * slot_length, features)[flat_index]  21.2 us
    all_to_all x1, waiting for transfers between devices, local(): lax.all_to_all(out_slots, 'req', split_axis=0, concat_axis=0, tiled=True)  20.9 us
    dot_general x1, matrix products, local(): jnp.dot(hidden, w_down, preferred_element_type=jnp.float32)  11.4 us
  transfers between devices with their start and end apart: 5, of which 4 were waited for; matrix products, arithmetic and copies ran while one was open for 3% of the time, Pallas kernels for 0%

commit v1 on v0

--- a/solution.py
+++ b/solution.py
@@ -84,7 +84,16 @@
     tail_offset = wanted - block_id * block_len
     trailing = prefix_cache.shape[2:]
     initial = jnp.zeros((attach_slots.shape[0], window) + trailing, jnp.bfloat16)
-    shard_rows = lax.all_gather(prefix_cache, "req", axis=0, tiled=True)
+    ways = lax.axis_size("req")
+    up = [(d, (d + 1) % ways) for d in range(ways)]
+    down = [(d, (d - 1) % ways) for d in range(ways)]
+    earlier, later = ([prefix_cache], [prefix_cache])
+    for _ in range(ways // 2):
+        earlier.append(lax.ppermute(earlier[-1], "req", up))
+    for _ in range((ways - 1) // 2):
+        later.append(lax.ppermute(later[-1], "req", down))
+    line = jnp.concatenate([*earlier[::-1], *later[1:]], axis=0)
+    shard_rows = jnp.roll(line, (lax.axis_index("req") - ways // 2) * prefix_cache.shape[0], axis=0)
     held_blocks = shard_rows.shape[0]
     flat_rows = shard_rows.reshape((held_blocks * block_len,) + trailing)
     inside = (tail_store >= 0) & (tail_store < held_blocks)

time: 540 us -> 568 us (1.052)
  starting transfers between devices: 15 us -> 70 us
  waiting for transfers between devices: 326 us -> 287 us
  local copies, waits for them, and re-layouts: 103 us -> 112 us
    all_gather x1 -> x0, waiting for transfers between devices: 176 us -> none  [fetch_prefix(): shard_rows = lax.all_gather(prefix_cache, 'req', axis=0, tiled=True)]
    ppermute x0 -> x15, waiting for transfers between devices: none -> 140 us  [the longest x8 134 us: fetch_prefix(): earlier.append(lax.ppermute(earlier[-1], 'req', up))]
    ppermute x0 -> x15, starting transfers between devices: none -> 55.2 us  [the longest x7 44.5 us: fetch_prefix(): later.append(lax.ppermute(later[-1], 'req', down))]
    unnamed x28 -> x83, local copies, waits for them, and re-layouts: 9.1 us -> 27.7 us
    gather x3, local copies, waits for them, and re-layouts: 27.8 us -> 16.3 us  [to_slots(): return values[slot_source].reshape((peers, slot_length) + values.shape[1:])]
  transfers between devices with their start and end apart: 5 -> 19, of which waited for: 4 -> 14; matrix products, arithmetic and copies ran while one was open for 3% -> 7% of each run, Pallas kernels for 0% -> 0%
where the time goes in v1:
time: 568 us; the launch traced here: 559 us
  waiting for transfers between devices  287 us (51%)
  local copies, waits for them, and re-layouts  112 us (20%)
  starting transfers between devices  70 us (12%)
  matrix products  40.7 us (7%)
  other arithmetic  35.1 us (6%)
  between operations  14.2 us (2%)
    ppermute x8, waiting for transfers between devices, fetch_prefix(): earlier.append(lax.ppermute(earlier[-1], 'req', up))  134 us
    psum x1, waiting for transfers between devices, local(): lax.psum(partial_value.astype(jnp.bfloat16), 'tp').astype(jnp.float32)  89.6 us
    ppermute x7, starting transfers between devices, fetch_prefix(): later.append(lax.ppermute(later[-1], 'req', down))  44.5 us
    reduce_scatter x1, waiting for transfers between devices, local(): lax.psum_scatter(jnp.dot(hidden, w_down, preferred_element_type=jnp.float...  36.9 us
    unnamed x83, local copies, waits for them, and re-layouts  27.7 us
    gather x2, local copies, waits for them, and re-layouts, local(): input_rows = landed.reshape(peers * slot_length, features)[flat_index]  21.2 us
    all_to_all x1, waiting for transfers between devices, local(): lax.all_to_all(out_slots, 'req', split_axis=0, concat_axis=0, tiled=True)  20.8 us
    gather x3, local copies, waits for them, and re-layouts, to_slots(): return values[slot_source].reshape((peers, slot_length) + values.shape[1:])  16.3 us
  transfers between devices with their start and end apart: 19, of which 14 were waited for; matrix products, arithmetic and copies ran while one was open for 7% of the time, Pallas kernels for 0%

profile of v1, /device:TPU:7, one launch (start us, length us, event | category | flops | bytes accessed | tf_op | source)
XLA Modules:
  0.0 559.3 jit_solution(17251441327597955503)
XLA Ops:
  7.5 9.7 %gather_fusion = bf16[16,112,2880]{2,1,0:T(8,128)(2,1)} fusion(bf16[16,112,2880]{2,1,0:T(8,128)(2,1)} %param.15, s32[1024]{0:T(1024)S(1)} %pad_clamp_fusion.3), kind=kCustom, calls=%fused_computation | custom fusion | bytes 20643904 | tf_op jit(solution)/shard_map/gather | solution.py:155
  17.2 8.0 %all-to-all-start = ((bf16[16,112,2880]{2,1,0:T(8,128)(2,1)}), bf16[16,112,2880]{2,1,0:T(8,128)(2,1)}, u32[]{:S(2)}, u32[]{:S(2)}) async-start(bf16[16,112,2880]{2,1,0:T(8,128)(2,1)} %gather_fusion), calls=%async_computation | async-start | bytes 21102592 | tf_op jit(solution)/shard_map/all_to_all | solution.py:154
  25.2 1.4 collective-permute-start
  26.6 3.5 collective-permute-start.8
  32.2 2.5 multiply_cosine_fusion
  35.4 118.0 %collective-permute-done = bf16[4,128,1,128]{3,1,2,0:T(8,128)(2,1)S(1)} collective-permute-done((bf16[4,128,1,128]{3,1,2,0:T(8,128)(2,1)S(1)}, bf16[4,128,1,128]{3,1,2,0:T(8,128)(2,1)S(1)}, u32[]{:S(2)}, u32[]{:S(2)}) %collective-permute-start) | collective-permute-done | bytes 131104 | tf_op jit(solution)/shard_map/ppermute | solution.py:92
  153.4 7.1 %collective-permute-done.1 = bf16[4,128,1,128]{3,1,2,0:T(8,128)(2,1)S(1)} collective-permute-done((bf16[4,128,1,128]{3,1,2,0:T(8,128)(2,1)S(1)}, bf16[4,128,1,128]{3,1,2,0:T(8,128)(2,1)S(1)}, u32[]{:S(2)}, u32[]{:S(2)}) %collective-permute-start.1) | collective-permute-done | bytes 131104 | tf_op jit(solution)/shard_map/ppermute | solution.py:92
  160.5 1.2 collective-permute-done.8
  161.7 7.8 %collective-permute-start.9 = (bf16[4,128,1,128]{3,1,2,0:T(8,128)(2,1)S(1)}, bf16[4,128,1,128]{3,1,2,0:T(8,128)(2,1)}, u32[]{:S(2)}, u32[]{:S(2)}) collective-permute-start(bf16[4,128,1,128]{3,1,2,0:T(8,128)(2,1)S(1)} %collective-permute-done.8), channel_id=1, source_target_pairs={{0,120},{8,0},{16,8},{24,16},{32,24},{40,32},{48,40},{56,48},{64,5... | collective-permute-start | bytes 393224 | tf_op jit(solution)/shard_map/ppermute | solution.py:94
  169.7 1.7 collective-permute-done.9
  171.4 6.7 %collective-permute-start.10 = (bf16[4,128,1,128]{3,1,2,0:T(8,128)(2,1)}, bf16[4,128,1,128]{3,1,2,0:T(8,128)(2,1)S(1)}, u32[]{:S(2)}, u32[]{:S(2)}) collective-permute-start(bf16[4,128,1,128]{3,1,2,0:T(8,128)(2,1)} %collective-permute-done.9), channel_id=1, source_target_pairs={{0,120},{8,0},{16,8},{24,16},{32,24},{40,32},{48,40},{56,48},{64,5... | collective-permute-start | bytes 393224 | tf_op jit(solution)/shard_map/ppermute | solution.py:94
  178.1 7.3 %collective-permute-done.3 = bf16[4,128,1,128]{3,1,2,0:T(8,128)(2,1)} collective-permute-done((bf16[4,128,1,128]{3,1,2,0:T(8,128)(2,1)}, bf16[4,128,1,128]{3,1,2,0:T(8,128)(2,1)}, u32[]{:S(2)}, u32[]{:S(2)}) %collective-permute-start.3) | collective-permute-done | bytes 131104 | tf_op jit(solution)/shard_map/ppermute | solution.py:92
  185.4 2.5 collective-permute-start.4
  189.5 2.3 collective-permute-start.11
  191.8 0.9 collective-permute-done.4
  192.8 6.9 %collective-permute-start.5 = (bf16[4,128,1,128]{3,1,2,0:T(8,128)(2,1)S(1)}, bf16[4,128,1,128]{3,1,2,0:T(8,128)(2,1)S(1)}, u32[]{:S(2)}, u32[]{:S(2)}) collective-permute-start(bf16[4,128,1,128]{3,1,2,0:T(8,128)(2,1)S(1)} %collective-permute-done.4), channel_id=1, source_target_pairs={{0,8},{8,16},{16,24},{24,32},{32,40},{40,48},{48,56},{56,64},{64,7... | collective-permute-start | bytes 393224 | tf_op jit(solution)/shard_map/ppermute | solution.py:92
  201.0 12.5 %collective-permute-start.12 = (bf16[4,128,1,128]{3,1,2,0:T(8,128)(2,1)S(1)}, bf16[4,128,1,128]{3,1,2,0:T(8,128)(2,1)}, u32[]{:S(2)}, u32[]{:S(2)}) collective-permute-start(bf16[4,128,1,128]{3,1,2,0:T(8,128)(2,1)S(1)} %collective-permute-done.11), channel_id=1, source_target_pairs={{0,120},{8,0},{16,8},{24,16},{32,24},{40,32},{48,40},{56,48},{64,5... | collective-permute-start | bytes 393224 | tf_op jit(solution)/shard_map/ppermute | solution.py:94
  213.7 1.8 collective-permute-done.12
  215.5 5.7 %collective-permute-start.13 = (bf16[4,128,1,128]{3,1,2,0:T(8,128)(2,1)}, bf16[4,128,1,128]{3,1,2,0:T(8,128)(2,1)}, u32[]{:S(2)}, u32[]{:S(2)}) collective-permute-start(bf16[4,128,1,128]{3,1,2,0:T(8,128)(2,1)} %collective-permute-done.12), channel_id=1, source_target_pairs={{0,120},{8,0},{16,8},{24,16},{32,24},{40,32},{48,40},{56,48},{64,5... | collective-permute-start | bytes 393224 | tf_op jit(solution)/shard_map/ppermute | solution.py:94
  222.3 1.1 collective-permute-done.13
  223.4 6.1 %collective-permute-start.14 = (bf16[4,128,1,128]{3,1,2,0:T(8,128)(2,1)}, bf16[4,128,1,128]{3,1,2,0:T(8,128)(2,1)S(1)}, u32[]{:S(2)}, u32[]{:S(2)}) collective-permute-start(bf16[4,128,1,128]{3,1,2,0:T(8,128)(2,1)} %collective-permute-done.13), channel_id=1, source_target_pairs={{0,120},{8,0},{16,8},{24,16},{32,24},{40,32},{48,40},{56,48},{64,5... | collective-permute-start | bytes 393224 | tf_op jit(solution)/shard_map/ppermute | solution.py:94
  231.8 0.9 constant_dynamic-update-slice_fusion.29
  234.6 0.9 constant_dynamic-update-slice_fusion.26
  237.5 0.9 constant_dynamic-update-slice_fusion.19
  238.4 0.9 constant_dynamic-update-slice_fusion.18
  239.3 0.9 constant_dynamic-update-slice_fusion.17
  240.3 0.9 constant_dynamic-update-slice_fusion.15
  247.1 1.5 constant_dynamic-slice_fusion
  248.5 7.9 %gather_fusion.2 = bf16[2048,128]{1,0:T(8,128)(2,1)S(1)} fusion(bf16[8192,128]{1,0:T(8,128)(2,1)} %bitcast.89, s32[2048]{0:T(1024)S(1)} %get-tuple-element.19), kind=kCustom, calls=%fused_computation.2 | custom fusion | bytes 1056768 | tf_op jit(solution)/shard_map/gather | solution.py:100
  256.5 1.0 copy.34
  257.5 1.9 broadcast_select_fusion.1
  259.3 14.6 %gather_fusion.1 = bf16[768,2880]{1,0:T(8,128)(2,1)} fusion(bf16[1792,2880]{1,0:T(8,128)(2,1)} %bitcast.4, s32[1024]{0:T(1024)S(1)} %pad_clamp_fusion.2), kind=kCustom, calls=%fused_computation.1 | custom fusion | bytes 8850432 | tf_op jit(solution)/shard_map/gather | solution.py:157
  274.0 6.6 %copy.33 = bf16[768,2880]{0,1:T(8,128)(2,1)} copy(bf16[768,2880]{1,0:T(8,128)(2,1)} %gather_fusion.1) | data formatting | bytes 8847360 | tf_op jit(solution)/shard_map/gather | solution.py:157
  280.6 3.3 fusion.5
  284.2 2.6 fusion.24
  287.5 4.6 gather_fusion.3
  292.1 2.0 copy.36
  294.1 6.1 %fusion.20 = f32[768,512]{0,1:T(8,128)S(1)} fusion(bf16[2880,512]{1,0:T(8,128)(2,1)} %param.23, bf16[768,2880]{0,1:T(8,128)(2,1)} %copy.33, f32[2880]{0:T(1024)S(1)} %copy-done.15, f32[768]{0:T(1024)S(1)} %add_rsqrt_fusion.1), kind=kOutput, calls=%fused_computation.40 | convolution fusion | flops 2273771520 | bytes 8960256 | tf_op jit(solution)/shard_map/dot_general | solution.py:160
  300.2 1.3 fusion.69
  301.5 3.2 copy.50
  304.7 3.4 copy.51
  308.1 3.7 subtract_convert_fusion
  311.7 2.1 pad_maximum_fusion
  313.9 5.7 %gather_fusion.4 = bf16[1792,8,64]{2,1,0:T(8,128)(2,1)} fusion(bf16[768,8,64]{2,1,0:T(8,128)(2,1)} %pad_maximum_fusion, s32[2048]{0:T(1024)S(1)} %get-tuple-element.20), kind=kCustom, calls=%fused_computation.4 | custom fusion | bytes 3677184 | tf_op jit(solution)/shard_map/gather | solution.py:151
  319.6 5.1 fusion.1
  324.8 5.3 fusion
  330.2 6.6 %convert_bitcast_fusion = bf16[16,112,1,8,64]{1,4,3,0,2:T(8,128)(2,1)} fusion(f32[16,8,112]{2,1,0:T(8,128)S(1)} %exponential_add_fusion, f32[16,8,112]{2,1,0:T(8,128)S(1)} %broadcast_maximum_fusion, f32[16,240,112,8]{1,2,3,0:T(8,128)S(1)} %get-tuple-element.18, pred[112,240]{1,0:T(8,128)(4,1)S(1)} %fusion.41, bf16[16,128,1,128]{1,3,0,2:T(8,128)(2,1)S(1)} %copy-done.3, ...), kind=kOutput, calls=%fused_computation.34 | convolution fusion | flops 459505664 | bytes 16722176 | tf_op jit(solution)/shard_map/nkgts,nskd->ntkgd/dot_general | solution.py:63
  336.8 4.8 copy.48
  341.6 5.9 %reshape.650 = bf16[1792,512]{1,0:T(8,128)(2,1)} reshape(bf16[16,112,1,8,64]{4,3,1,0,2:T(8,128)(2,1)} %copy.48) | data formatting | bytes 3670016 | tf_op jit(solution)/shard_map/reshape | solution.py:69
  347.5 5.3 gather_fusion.5
  352.8 5.7 %convolution_convert_fusion = bf16[768,2880]{0,1:T(8,128)(2,1)} fusion(bf16[768,512]{1,0:T(8,128)(2,1)} %gather_fusion.5, bf16[512,2880]{0,1:T(8,128)(2,1)S(1)} %copy-done), kind=kOutput, calls=%fused_computation.28 | convolution fusion | flops 2267136000 | bytes 8159232 | tf_op jit(solution)/shard_map/dot_general | solution.py:170
  359.2 89.6 %all-reduce.2.cloned.1.call-done = bf16[768,2880]{0,1:T(8,128)(2,1)} async-done(((bf16[768,2880]{0,1:T(8,128)(2,1)}), bf16[768,2880]{0,1:T(8,128)(2,1)}) %all-reduce.2.cloned.1.call-update) | async-done | bytes 4423696 | tf_op jit(solution)/shard_map/psum | solution.py:171
  448.8 5.5 fusion.2
  454.3 2.0 copy-done.2
  456.3 3.2 fusion.18
  459.6 11.3 %convolution_convert_fusion.1 = bf16[768,2880]{0,1:T(8,128)(2,1)} fusion(bf16[360,2880]{1,0:T(8,128)(2,1)} %param.29, bf16[2880,360]{0,1:T(8,128)(2,1)} %param.28, bf16[768,2880]{0,1:T(8,128)(2,1)} %copy-done.2, f32[2880]{0:T(1024)S(1)} %convert_element_type.103, f32[768]{0:T(1024)S(1)} %add_rsqrt_fusion, f32[768,360]{0,1:T(8,128)} %fusion.18), kind=kOutput, calls=%fused_computation.29 | convolution fusion | flops 3197767680 | bytes 14115072 | tf_op jit(solution)/shard_map/dot_general | solution.py:181
  471.7 36.9 %reduce-scatter.2.cloned.1.call-done = bf16[768,360]{0,1:T(8,128)(2,1)} async-done(((bf16[768,2880]{0,1:T(8,128)(2,1)}), bf16[768,360]{0,1:T(8,128)(2,1)}) %reduce-scatter.2.cloned.1.call-update) | async-done | bytes 552976 | tf_op jit(solution)/shard_map/reduce_scatter | solution.py:180
  508.6 2.1 add_convert_fusion.1
  510.7 1.4 copy.43
  512.1 6.0 %gather_fusion.6 = bf16[1792,360]{1,0:T(8,128)(2,1)} fusion(bf16[768,360]{1,0:T(8,128)(2,1)S(1)} %copy.43, s32[2048]{0:T(1024)S(1)} %get-tuple-element.20), kind=kCustom, calls=%fused_computation.6 | custom fusion | bytes 2587648 | tf_op jit(solution)/shard_map/gather | solution.py:151
  518.1 2.7 broadcast_select_fusion
  520.8 6.7 %all-to-all-start.1 = ((bf16[16,112,360]{2,1,0:T(8,128)(2,1)}), bf16[16,112,360]{2,1,0:T(8,128)(2,1)}, u32[]{:S(2)}, u32[]{:S(2)}) async-start(bf16[16,112,360]{2,1,0:T(8,128)(2,1)} %broadcast_select_fusion), calls=%async_computation.2 | async-start | bytes 2752512 | tf_op jit(solution)/shard_map/all_to_all | solution.py:188
  528.2 20.8 %all-to-all-done.1 = bf16[16,112,360]{2,1,0:T(8,128)(2,1)} async-done(((bf16[16,112,360]{2,1,0:T(8,128)(2,1)}), bf16[16,112,360]{2,1,0:T(8,128)(2,1)}, u32[]{:S(2)}, u32[]{:S(2)}) %all-to-all-start.1) | async-done | bytes 1290272 | tf_op jit(solution)/shard_map/all_to_all | solution.py:188
  549.1 3.2 gather_fusion.7
  (137 shorter events, 23.4 us)
Async XLA Ops:
  6.5 346.3 %copy-start = (bf16[512,2880]{0,1:T(8,128)(2,1)S(1)}, bf16[512,2880]{0,1:T(8,128)(2,1)}, u32[]{:S(2)}) copy-start(bf16[512,2880]{0,1:T(8,128)(2,1)} %param.25) | copy-start | bytes 8847364
  17.2 8.0 %copy-start.6 = (bf16[4,128,1,128]{3,1,2,0:T(8,128)(2,1)S(1)}, bf16[4,128,1,128]{3,1,2,0:T(8,128)(2,1)}, u32[]{:S(2)}) copy-start(bf16[4,128,1,128]{3,1,2,0:T(8,128)(2,1)} %param.19) | copy-start | bytes 393220
  17.2 13.8 %copy-start.23 = (s32[256]{0:T(256)S(1)}, s32[256]{0:T(256)}, u32[]{:S(2)}) copy-start(s32[256]{0:T(256)} %param.18) | copy-start | bytes 3076
  17.2 13.9 %copy-start.16 = (s32[16,16]{1,0:T(8,128)S(1)}, s32[16,16]{1,0:T(8,128)}, u32[]{:S(2)}) copy-start(s32[16,16]{1,0:T(8,128)} %param.17) | copy-start | bytes 3076
  17.2 204.5 %copy-start.17 = (bf16[2880]{0:T(1024)(128)(2,1)S(1)}, bf16[2880]{0:T(1024)(128)(2,1)}, u32[]{:S(2)}) copy-start(bf16[2880]{0:T(1024)(128)(2,1)} %param.22) | copy-start | bytes 17284
  17.2 242.2 %all-to-all-start = ((bf16[16,112,2880]{2,1,0:T(8,128)(2,1)}), bf16[16,112,2880]{2,1,0:T(8,128)(2,1)}, u32[]{:S(2)}, u32[]{:S(2)}) async-start(bf16[16,112,2880]{2,1,0:T(8,128)(2,1)} %gather_fusion), calls=%async_computation | async-start | bytes 21102592 | tf_op jit(solution)/shard_map/all_to_all | solution.py:154
  25.1 423.7 %all-reduce.2.cloned.1.call-start = ((), (), s32[]{:S(2)}) async-start(), calls=%async_computation.3 | async-start | bytes 8847360 | tf_op jit(solution)/shard_map/psum | solution.py:171
  25.2 128.2 %collective-permute-start = (bf16[4,128,1,128]{3,1,2,0:T(8,128)(2,1)S(1)}, bf16[4,128,1,128]{3,1,2,0:T(8,128)(2,1)S(1)}, u32[]{:S(2)}, u32[]{:S(2)}) collective-permute-start(bf16[4,128,1,128]{3,1,2,0:T(8,128)(2,1)S(1)} %copy-done.6), channel_id=1, source_target_pairs={{0,8},{8,16},{16,24},{24,32},{32,40},{40,48},{48,56},{56,64},{64,7... | collective-permute-start | bytes 393224 | tf_op jit(solution)/shard_map/ppermute | solution.py:92
  26.6 135.1 %collective-permute-start.8 = (bf16[4,128,1,128]{3,1,2,0:T(8,128)(2,1)S(1)}, bf16[4,128,1,128]{3,1,2,0:T(8,128)(2,1)S(1)}, u32[]{:S(2)}, u32[]{:S(2)}) collective-permute-start(bf16[4,128,1,128]{3,1,2,0:T(8,128)(2,1)S(1)} %copy-done.6), channel_id=1, source_target_pairs={{0,120},{8,0},{16,8},{24,16},{32,24},{40,32},{48,40},{56,48},{64,5... | collective-permute-start | bytes 393224 | tf_op jit(solution)/shard_map/ppermute | solution.py:94
  31.1 122.3 %copy-start.21 = (f32[32]{0:T(128)}, f32[32]{0:T(128)S(1)}, u32[]{:S(2)}) copy-start(f32[32]{0:T(128)S(1)} %negate_power_fusion) | copy-start | bytes 388
  153.4 7.1 %collective-permute-start.1 = (bf16[4,128,1,128]{3,1,2,0:T(8,128)(2,1)S(1)}, bf16[4,128,1,128]{3,1,2,0:T(8,128)(2,1)S(1)}, u32[]{:S(2)}, u32[]{:S(2)}) collective-permute-start(bf16[4,128,1,128]{3,1,2,0:T(8,128)(2,1)S(1)} %collective-permute-done), channel_id=1, source_target_pairs={{0,8},{8,16},{16,24},{24,32},{32,40},{40,48},{48,56},{56,64},{64,7... | collective-permute-start | bytes 393224 | tf_op jit(solution)/shard_map/ppermute | solution.py:92
  160.5 9.0 %collective-permute-start.2 = (bf16[4,128,1,128]{3,1,2,0:T(8,128)(2,1)S(1)}, bf16[4,128,1,128]{3,1,2,0:T(8,128)(2,1)}, u32[]{:S(2)}, u32[]{:S(2)}) collective-permute-start(bf16[4,128,1,128]{3,1,2,0:T(8,128)(2,1)S(1)} %collective-permute-done.1), channel_id=1, source_target_pairs={{0,8},{8,16},{16,24},{24,32},{32,40},{40,48},{48,56},{56,64},{64,7... | collective-permute-start | bytes 393224 | tf_op jit(solution)/shard_map/ppermute | solution.py:92
  160.5 9.1 %copy-start.20 = (s32[16]{0:T(128)}, s32[16]{0:T(128)S(1)}, u32[]{:S(2)}) copy-start(s32[16]{0:T(128)S(1)} %broadcast_add_fusion) | copy-start | bytes 196
  161.7 9.8 %collective-permute-start.9 = (bf16[4,128,1,128]{3,1,2,0:T(8,128)(2,1)S(1)}, bf16[4,128,1,128]{3,1,2,0:T(8,128)(2,1)}, u32[]{:S(2)}, u32[]{:S(2)}) collective-permute-start(bf16[4,128,1,128]{3,1,2,0:T(8,128)(2,1)S(1)} %collective-permute-done.8), channel_id=1, source_target_pairs={{0,120},{8,0},{16,8},{24,16},{32,24},{40,32},{48,40},{56,48},{64,5... | collective-permute-start | bytes 393224 | tf_op jit(solution)/shard_map/ppermute | solution.py:94
  169.5 15.9 %collective-permute-start.3 = (bf16[4,128,1,128]{3,1,2,0:T(8,128)(2,1)}, bf16[4,128,1,128]{3,1,2,0:T(8,128)(2,1)}, u32[]{:S(2)}, u32[]{:S(2)}) collective-permute-start(bf16[4,128,1,128]{3,1,2,0:T(8,128)(2,1)} %collective-permute-done.2), channel_id=1, source_target_pairs={{0,8},{8,16},{16,24},{24,32},{32,40},{40,48},{48,56},{56,64},{64,7... | collective-permute-start | bytes 393224 | tf_op jit(solution)/shard_map/ppermute | solution.py:92
  171.4 17.4 %collective-permute-start.10 = (bf16[4,128,1,128]{3,1,2,0:T(8,128)(2,1)}, bf16[4,128,1,128]{3,1,2,0:T(8,128)(2,1)S(1)}, u32[]{:S(2)}, u32[]{:S(2)}) collective-permute-start(bf16[4,128,1,128]{3,1,2,0:T(8,128)(2,1)} %collective-permute-done.9), channel_id=1, source_target_pairs={{0,120},{8,0},{16,8},{24,16},{32,24},{40,32},{48,40},{56,48},{64,5... | collective-permute-start | bytes 393224 | tf_op jit(solution)/shard_map/ppermute | solution.py:94
  185.4 7.3 %collective-permute-start.4 = (bf16[4,128,1,128]{3,1,2,0:T(8,128)(2,1)}, bf16[4,128,1,128]{3,1,2,0:T(8,128)(2,1)S(1)}, u32[]{:S(2)}, u32[]{:S(2)}) collective-permute-start(bf16[4,128,1,128]{3,1,2,0:T(8,128)(2,1)} %collective-permute-done.3), channel_id=1, source_target_pairs={{0,8},{8,16},{16,24},{24,32},{32,40},{40,48},{48,56},{56,64},{64,7... | collective-permute-start | bytes 393224 | tf_op jit(solution)/shard_map/ppermute | solution.py:92
  188.8 0.7 copy-start.7
  189.5 10.9 %collective-permute-start.11 = (bf16[4,128,1,128]{3,1,2,0:T(8,128)(2,1)S(1)}, bf16[4,128,1,128]{3,1,2,0:T(8,128)(2,1)S(1)}, u32[]{:S(2)}, u32[]{:S(2)}) collective-permute-start(bf16[4,128,1,128]{3,1,2,0:T(8,128)(2,1)S(1)} %collective-permute-done.10), channel_id=1, source_target_pairs={{0,120},{8,0},{16,8},{24,16},{32,24},{40,32},{48,40},{56,48},{64,5... | collective-permute-start | bytes 393224 | tf_op jit(solution)/shard_map/ppermute | solution.py:94
  192.8 22.7 %copy-start.11 = (bf16[4,128,1,128]{3,1,2,0:T(8,128)(2,1)}, bf16[4,128,1,128]{3,1,2,0:T(8,128)(2,1)S(1)}, u32[]{:S(2)}) copy-start(bf16[4,128,1,128]{3,1,2,0:T(8,128)(2,1)S(1)} %collective-permute-done.4) | copy-start | bytes 393220
  192.8 20.9 %collective-permute-start.5 = (bf16[4,128,1,128]{3,1,2,0:T(8,128)(2,1)S(1)}, bf16[4,128,1,128]{3,1,2,0:T(8,128)(2,1)S(1)}, u32[]{:S(2)}, u32[]{:S(2)}) collective-permute-start(bf16[4,128,1,128]{3,1,2,0:T(8,128)(2,1)S(1)} %collective-permute-done.4), channel_id=1, source_target_pairs={{0,8},{8,16},{16,24},{24,32},{32,40},{40,48},{48,56},{56,64},{64,7... | collective-permute-start | bytes 393224 | tf_op jit(solution)/shard_map/ppermute | solution.py:92
  200.4 0.7 copy-start.9
  201.0 14.5 %collective-permute-start.12 = (bf16[4,128,1,128]{3,1,2,0:T(8,128)(2,1)S(1)}, bf16[4,128,1,128]{3,1,2,0:T(8,128)(2,1)}, u32[]{:S(2)}, u32[]{:S(2)}) collective-permute-start(bf16[4,128,1,128]{3,1,2,0:T(8,128)(2,1)S(1)} %collective-permute-done.11), channel_id=1, source_target_pairs={{0,120},{8,0},{16,8},{24,16},{32,24},{40,32},{48,40},{56,48},{64,5... | collective-permute-start | bytes 393224 | tf_op jit(solution)/shard_map/ppermute | solution.py:94
  213.7 7.5 %copy-start.13 = (bf16[4,128,1,128]{3,1,2,0:T(8,128)(2,1)}, bf16[4,128,1,128]{3,1,2,0:T(8,128)(2,1)S(1)}, u32[]{:S(2)}) copy-start(bf16[4,128,1,128]{3,1,2,0:T(8,128)(2,1)S(1)} %collective-permute-done.5) | copy-start | bytes 393220
  213.7 8.0 %collective-permute-start.6 = (bf16[4,128,1,128]{3,1,2,0:T(8,128)(2,1)S(1)}, bf16[4,128,1,128]{3,1,2,0:T(8,128)(2,1)}, u32[]{:S(2)}, u32[]{:S(2)}) collective-permute-start(bf16[4,128,1,128]{3,1,2,0:T(8,128)(2,1)S(1)} %collective-permute-done.5), channel_id=1, source_target_pairs={{0,8},{8,16},{16,24},{24,32},{32,40},{40,48},{48,56},{56,64},{64,7... | collective-permute-start | bytes 393224 | tf_op jit(solution)/shard_map/ppermute | solution.py:92
  215.5 7.9 %collective-permute-start.13 = (bf16[4,128,1,128]{3,1,2,0:T(8,128)(2,1)}, bf16[4,128,1,128]{3,1,2,0:T(8,128)(2,1)}, u32[]{:S(2)}, u32[]{:S(2)}) collective-permute-start(bf16[4,128,1,128]{3,1,2,0:T(8,128)(2,1)} %collective-permute-done.12), channel_id=1, source_target_pairs={{0,120},{8,0},{16,8},{24,16},{32,24},{40,32},{48,40},{56,48},{64,5... | collective-permute-start | bytes 393224 | tf_op jit(solution)/shard_map/ppermute | solution.py:94
  221.7 8.3 %collective-permute-start.7 = (bf16[4,128,1,128]{3,1,2,0:T(8,128)(2,1)}, bf16[4,128,1,128]{3,1,2,0:T(8,128)(2,1)}, u32[]{:S(2)}, u32[]{:S(2)}) collective-permute-start(bf16[4,128,1,128]{3,1,2,0:T(8,128)(2,1)} %collective-permute-done.6), channel_id=1, source_target_pairs={{0,8},{8,16},{16,24},{24,32},{32,40},{40,48},{48,56},{56,64},{64,7... | collective-permute-start | bytes 393224 | tf_op jit(solution)/shard_map/ppermute | solution.py:92
  222.3 19.9 %copy-start.14 = (bf16[4,128,1,128]{3,1,2,0:T(8,128)(2,1)S(1)}, bf16[4,128,1,128]{3,1,2,0:T(8,128)(2,1)}, u32[]{:S(2)}) copy-start(bf16[4,128,1,128]{3,1,2,0:T(8,128)(2,1)} %copy-done.13) | copy-start | bytes 393220
  222.3 19.9 %copy-start.12 = (bf16[4,128,1,128]{3,1,2,0:T(8,128)(2,1)S(1)}, bf16[4,128,1,128]{3,1,2,0:T(8,128)(2,1)}, u32[]{:S(2)}) copy-start(bf16[4,128,1,128]{3,1,2,0:T(8,128)(2,1)} %copy-done.11) | copy-start | bytes 393220
  222.3 22.8 %copy-start.8 = (bf16[4,128,1,128]{3,1,2,0:T(8,128)(2,1)S(1)}, bf16[4,128,1,128]{3,1,2,0:T(8,128)(2,1)}, u32[]{:S(2)}) copy-start(bf16[4,128,1,128]{3,1,2,0:T(8,128)(2,1)} %copy-done.7) | copy-start | bytes 393220
  222.3 22.9 %copy-start.10 = (bf16[4,128,1,128]{3,1,2,0:T(8,128)(2,1)S(1)}, bf16[4,128,1,128]{3,1,2,0:T(8,128)(2,1)}, u32[]{:S(2)}) copy-start(bf16[4,128,1,128]{3,1,2,0:T(8,128)(2,1)} %copy-done.9) | copy-start | bytes 393220
  223.4 16.8 %collective-permute-start.14 = (bf16[4,128,1,128]{3,1,2,0:T(8,128)(2,1)}, bf16[4,128,1,128]{3,1,2,0:T(8,128)(2,1)S(1)}, u32[]{:S(2)}, u32[]{:S(2)}) collective-permute-start(bf16[4,128,1,128]{3,1,2,0:T(8,128)(2,1)} %collective-permute-done.13), channel_id=1, source_target_pairs={{0,120},{8,0},{16,8},{24,16},{32,24},{40,32},{48,40},{56,48},{64,5... | collective-permute-start | bytes 393224 | tf_op jit(solution)/shard_map/ppermute | solution.py:94
  280.6 3.6 copy-start.1
  280.6 3.6 copy-start.15
  284.2 2.6 copy-start.22
  301.5 6.6 %copy-start.5 = (f32[768,32]{1,0:T(8,128)S(1)}, f32[768,32]{1,0:T(8,128)}, u32[]{:S(2)}) copy-start(f32[768,32]{1,0:T(8,128)} %get-tuple-element.15) | copy-start | bytes 294916
  313.9 5.7 %copy-start.3 = (bf16[16,128,1,128]{1,3,0,2:T(8,128)(2,1)S(1)}, bf16[16,128,1,128]{1,3,0,2:T(8,128)(2,1)}, u32[]{:S(2)}) copy-start(bf16[16,128,1,128]{1,3,0,2:T(8,128)(2,1)} %broadcast_select_fusion.1) | copy-start | bytes 1572868
  319.6 5.1 copy-start.19
  324.8 5.4 copy-start.4
  358.5 0.7 copy-start.18
  358.6 150.0 %reduce-scatter.2.cloned.1.call-start = ((), (), s32[]{:S(2)}) async-start(), calls=%async_computation.4 | async-start | bytes 4976640 | tf_op jit(solution)/shard_map/reduce_scatter | solution.py:180
  448.8 7.5 %copy-start.24 = (bf16[2880,360]{0,1:T(8,128)(2,1)S(1)}, bf16[2880,360]{0,1:T(8,128)(2,1)}, u32[]{:S(2)}) copy-start(bf16[2880,360]{0,1:T(8,128)(2,1)} %param.27) | copy-start | bytes 6220804
  454.3 2.0 copy-start.2
  520.8 28.2 %all-to-all-start.1 = ((bf16[16,112,360]{2,1,0:T(8,128)(2,1)}), bf16[16,112,360]{2,1,0:T(8,128)(2,1)}, u32[]{:S(2)}, u32[]{:S(2)}) async-start(bf16[16,112,360]{2,1,0:T(8,128)(2,1)} %broadcast_select_fusion), calls=%async_computation.2 | async-start | bytes 2752512 | tf_op jit(solution)/shard_map/all_to_all | solution.py:188
Sparse Core Ops, SparseCore 0:
  358.7 90.0 all-reduce.1
  471.1 37.4 reduce-scatter.1
